TPU v7x, 128 devices: a whole 4x4x4 slice. The times are simulated.
128 devices in a mesh: scan: 8 (over z, x_lo), det: 16 (over y, x_hi, core).
Axes of the slice: x: 4 (x_hi: 2, x_lo: 2; x = x_hi * 2 + x_lo), y: 4, z: 4, core: 2. Of those that a mesh axis runs over, the one named last changes fastest.
Arguments:
- frames: bfloat16 [16, 1024, 16384], P('det', 'scan'), may hold values from -6 to 6
- offsets: int32 [16384, 2], P(('scan', 'det')), may hold values from -32 to 32
- bright: int32 [16384], P(('scan', 'det')), may hold values from 0 to 1, as said below
- aberration: float32 [2], replicated, may hold values from 0.5 to 2
Outputs:
- tiles: float32 [16, 8, 160], P('det', 'scan')
Inputs may be any that keep to these rules, and one draw needn't show every extreme that they name: bright[k] is 1 exactly where (k // 128 - a)^2 + (k % 128 - b)^2 <= R^2 and 0 elsewhere, for one centre with whole a in 62 .. 66 and whole b in 62 .. 66, and one whole radius R in 40 .. 56, all ranges inclusive; so at least one pixel is 1.
All inputs are finite; a program needn't handle non-finite values.
Results may differ from a plain program's by a relative error of at most 0.0023.
Values may be sent and summed in bfloat16 or wider, within the bound.
No kernel may reach another device: no remote copies, remote signals or barrier semaphores. Data moves between devices by JAX's collectives and lax.ppermute only.
A program may use at most 128 MiB of HBM per device.

v0:
```python
import math
import jax
import jax.numpy as jnp
from jax import lax
from jax.sharding import PartitionSpec as P

SR = 16
SC = 1024
DROWS = 128
DCOLS = 128
HALO = 16
TWO_PI = 2.0 * math.pi
EXACT_PRECISION = lax.Precision.HIGHEST


def phase_angles(first, second_operand, modulus):
    product = jnp.mod(first[:, None] * second_operand[None, :], modulus)
    return TWO_PI / modulus * product.astype(jnp.float32)


def signed_frequency(length):
    position = jnp.arange(length, dtype=jnp.int32)
    folded = jnp.where(position < length // 2, position, position - length)
    return 2.0 * folded.astype(jnp.float32) / length


def pixel_phase(pixel_index, shifts, aberration):
    freq_rows = signed_frequency(SR)[:, None, None]
    freq_cols = signed_frequency(SC)[None, :, None]
    half_rows = DROWS // 2
    half_cols = DCOLS // 2
    tilt_x = ((pixel_index // DCOLS - half_rows).astype(jnp.float32) / half_rows)[None, None, :]
    tilt_y = ((pixel_index % DCOLS - half_cols).astype(jnp.float32) / half_cols)[None, None, :]
    ramp_rows = jnp.mod(jnp.arange(SR, dtype=jnp.int32)[:, None] * shifts[:, 0][None, :], SR)
    ramp_cols = jnp.mod(jnp.arange(SC, dtype=jnp.int32)[:, None] * shifts[:, 1][None, :], SC)
    shift_phase = (
        TWO_PI / SR * ramp_rows.astype(jnp.float32)[:, None, :]
        + TWO_PI / SC * ramp_cols.astype(jnp.float32)[None, :, :]
    )
    tilt_sq = tilt_x * tilt_x + tilt_y * tilt_y
    tilt_dot = tilt_x * freq_rows + tilt_y * freq_cols
    moved_x = freq_rows + tilt_x
    moved_y = freq_cols + tilt_y
    moved_sq = moved_x * moved_x + moved_y * moved_y
    lens_phase = math.pi * (
        aberration[0] * (freq_rows * freq_rows + freq_cols * freq_cols)
        + aberration[1] * (moved_sq * moved_sq - tilt_sq * tilt_sq - 4.0 * tilt_sq * tilt_dot)
    )
    return shift_phase - lens_phase


def window_weights(width):
    position = jnp.arange(width, dtype=jnp.int32)
    nearest = jnp.minimum(position, width - 1 - position)
    ramped = 0.3 + 0.35 * (
        1.0 - jnp.cos(math.pi * (nearest.astype(jnp.float32) + 0.5) / (2 * HALO))
    )
    return jnp.where(nearest < 2 * HALO, ramped, jnp.float32(1.0))


def inverse_transform(spec_real, spec_imag, columns, rows):
    col_angles = phase_angles(jnp.arange(SC, dtype=jnp.int32), columns, SC)
    cos_cols = jnp.cos(col_angles)
    sin_cols = jnp.sin(col_angles)
    real_piece = jnp.dot(spec_real, cos_cols, precision=EXACT_PRECISION) - jnp.dot(
        spec_imag, sin_cols, precision=EXACT_PRECISION
    )
    imaginary_piece = jnp.dot(spec_real, sin_cols, precision=EXACT_PRECISION) + jnp.dot(
        spec_imag, cos_cols, precision=EXACT_PRECISION
    )
    angles_by_row = phase_angles(jnp.arange(SR, dtype=jnp.int32), rows, SR)
    row_cosines = jnp.cos(angles_by_row)
    row_sines = jnp.sin(angles_by_row)
    return jnp.dot(row_cosines.T, real_piece, precision=EXACT_PRECISION) - jnp.dot(
        row_sines.T, imaginary_piece, precision=EXACT_PRECISION
    )


def local(frames, offsets, bright, aberration):
    scan_size = lax.axis_size("scan")
    det_size = lax.axis_size("det")
    rows_dev, tile, detector = frames.shape
    owned = offsets.shape[0]
    groups = detector // owned
    owner = lax.axis_index("scan") * det_size + lax.axis_index("det")
    blocks = jnp.transpose(frames.reshape(rows_dev * tile, groups, owned), (1, 0, 2))
    arrived = lax.all_to_all(blocks, ("scan", "det"), split_axis=0, concat_axis=0, tiled=True)
    images = arrived.reshape(scan_size, det_size, rows_dev, tile, owned)
    full_cols = jnp.arange(SC, dtype=jnp.int32)
    col_angles = phase_angles(full_cols, full_cols, SC)
    col_cos = jnp.cos(col_angles).astype(jnp.bfloat16)
    col_sin = jnp.sin(col_angles).astype(jnp.bfloat16)
    table = jnp.concatenate([col_cos, -col_sin], axis=1).reshape(scan_size, tile, 2 * SC)
    both_col = jnp.einsum(
        "abrcp,acq->brqp", images, table, preferred_element_type=jnp.float32
    ).reshape(SR, 2 * SC, owned)
    real_col = both_col[:, :SC]
    imag_col = both_col[:, SC:]
    full_rows = jnp.arange(SR, dtype=jnp.int32)
    angles_by_row = phase_angles(full_rows, full_rows, SR)
    row_cos = jnp.cos(angles_by_row)
    row_sin = jnp.sin(angles_by_row)
    real_full = jnp.einsum(
        "rs,rqp->sqp", row_cos, real_col, precision=EXACT_PRECISION
    ) + jnp.einsum("rs,rqp->sqp", row_sin, imag_col, precision=EXACT_PRECISION)
    imag_full = jnp.einsum(
        "rs,rqp->sqp", row_cos, imag_col, precision=EXACT_PRECISION
    ) - jnp.einsum("rs,rqp->sqp", row_sin, real_col, precision=EXACT_PRECISION)
    pixel_index = owner * owned + jnp.arange(owned, dtype=jnp.int32)
    phase = pixel_phase(pixel_index, offsets, aberration)
    weights = bright.astype(jnp.float32)
    turn_cos = jnp.cos(phase) * weights
    turn_sin = jnp.sin(phase) * weights
    spec_real = jnp.sum(real_full * turn_cos - imag_full * turn_sin, axis=2)
    spec_imag = jnp.sum(real_full * turn_sin + imag_full * turn_cos, axis=2)
    packed = jnp.concatenate(
        [spec_real.reshape(-1), spec_imag.reshape(-1), jnp.sum(weights).reshape(1)]
    )
    total = lax.psum(packed, ("scan", "det"))
    spec_real = total[: SR * SC].reshape(SR, SC)
    spec_imag = total[SR * SC : 2 * SR * SC].reshape(SR, SC)
    bright_sum = total[2 * SR * SC]
    width = tile + 2 * HALO
    columns = jnp.mod(lax.axis_index("scan") * tile - HALO + jnp.arange(width, dtype=jnp.int32), SC)
    rows = lax.axis_index("det") * rows_dev + jnp.arange(rows_dev, dtype=jnp.int32)
    picture = inverse_transform(spec_real, spec_imag, columns, rows)
    return (
        picture * (1.0 / (SR * SC)) / jnp.sqrt(bright_sum) * window_weights(width)[None, :]
    ).reshape(rows_dev, 1, width)


def solution(mesh):
    placed = (P("det", "scan", None), P(("scan", "det"), None), P(("scan", "det")), P())
    return jax.shard_map(
        local, mesh=mesh, in_specs=placed, out_specs=P("det", "scan", None), check_vma=False
    )
```

profile of v0, /device:TPU:1, one launch (start us, length us, event | category | flops | bytes accessed | tf_op | source)
XLA Modules:
  0.0 367.1 jit_solution(14988252802277870520)
XLA Ops:
  6.5 0.0 copy-start.5
  6.5 0.0 copy-start.3
  6.5 0.0 copy-start.4
  6.5 6.4 %copy.37 = bf16[1,128,16384]{1,2,0:T(8,128)(2,1)} copy(bf16[1,128,16384]{2,1,0:T(8,128)(2,1)} %param.4) | data formatting | bytes 8388608 | tf_op args[0]
  12.9 11.9 %all-to-all-start = ((bf16[128,128,128]{1,2,0:T(8,128)(2,1)}), bf16[128,128,128]{1,2,0:T(8,128)(2,1)}, u32[]{:S(2)}, u32[]{:S(2)}) async-start(bf16[128,128,128]{1,2,0:T(8,128)(2,1)} %bitcast.61), calls=%async_computation | async-start | bytes 8388608 | tf_op jit(solution)/shard_map/all_to_all | solution.py:87
  24.9 0.0 all-reduce.2.cloned.1.call-start
  24.9 0.0 copy-done.5
  25.0 0.0 copy-done.3
  25.0 0.7 fusion.126
  25.7 0.7 add_multiply_fusion.1
  26.4 0.2 copy.42
  26.7 0.6 convert_reduce_fusion
  27.3 0.0 copy-done.4
  27.3 0.1 add_multiply_fusion.2
  27.4 0.3 fusion.27
  27.6 1.2 add_multiply_fusion
  28.9 15.5 %cosine_convert_fusion = bf16[8,128,1024]{1,2,0:T(8,128)(2,1)S(1)} fusion(s32[8,128]{1,0:T(8,128)S(1)} %multiply_add_fusion), kind=kLoop, calls=%fused_computation.25 | loop fusion | flops 15728640 | bytes 2101248 | tf_op jit(solution)/shard_map/convert_element_type | solution.py:91
  44.3 16.9 %fusion.18 = bf16[8,128,1024]{1,2,0:T(8,128)(2,1)} fusion(s32[8,128]{1,0:T(8,128)S(1)} %multiply_add_fusion), kind=kLoop, calls=%fused_computation.29 | loop fusion | flops 18874368 | bytes 2101248 | tf_op jit(solution)/shard_map/neg | solution.py:93
  61.2 15.5 %all-to-all-done = bf16[128,128,128]{1,2,0:T(8,128)(2,1)} async-done(((bf16[128,128,128]{1,2,0:T(8,128)(2,1)}), bf16[128,128,128]{1,2,0:T(8,128)(2,1)}, u32[]{:S(2)}, u32[]{:S(2)}) %all-to-all-start) | async-done | bytes 4194336 | tf_op jit(solution)/shard_map/all_to_all | solution.py:87
  76.8 13.4 %convolution_bitcast_fusion = f32[16,2048,128]{2,1,0:T(8,128)} fusion(bf16[8,16,128,128]{2,3,1,0:T(8,128)(2,1)} %bitcast.5, bf16[8,128,1024]{1,2,0:T(8,128)(2,1)} %fusion.18, bf16[8,128,1024]{1,2,0:T(8,128)(2,1)S(1)} %cosine_convert_fusion), kind=kOutput, calls=%fused_computation.13 | convolution fusion | flops 8598323200 | bytes 25165824 | tf_op jit(solution)/shard_map/abrcp,acq->brqp/dot_general | solution.py:94
  90.2 6.9 %fusion.124 = (f32[16,1024,128]{2,1,0:T(8,128)S(1)}, f32[16,1024,128]{2,1,0:T(8,128)S(1)}) fusion(f32[16,2048,128]{2,1,0:T(8,128)} %convolution_bitcast_fusion), kind=kLoop, calls=%fused_computation.169 | loop fusion | bytes 33554432 | tf_op jit(solution)/shard_map/slice | solution.py:97
  97.1 11.6 %fusion.4 = f32[16,1024,128]{2,0,1:T(8,128)S(1)} fusion(f32[16,1024,128]{2,1,0:T(8,128)S(1)} %get-tuple-element.7), kind=kOutput, calls=%fused_computation.9 | convolution fusion | flops 402656768 | bytes 16777216 | tf_op jit(solution)/shard_map/rs,rqp->sqp/dot_general | solution.py:108
  108.7 16.6 %fusion.6 = f32[16,1024,128]{2,0,1:T(8,128)} fusion(f32[16,1024,128]{2,1,0:T(8,128)S(1)} %get-tuple-element.7), kind=kOutput, calls=%fused_computation.11 | convolution fusion | flops 402656768 | bytes 16777216 | tf_op jit(solution)/shard_map/rs,rqp->sqp/dot_general | solution.py:103
  125.3 0.0 copy-start
  125.3 0.0 copy-start.1
  125.3 0.0 copy-start.2
  125.3 16.6 %fusion.2 = f32[16,1024,128]{2,0,1:T(8,128)} fusion(f32[16,1024,128]{2,1,0:T(8,128)S(1)} %get-tuple-element.8), kind=kOutput, calls=%fused_computation.7 | convolution fusion | flops 402656768 | bytes 16777216 | tf_op jit(solution)/shard_map/rs,rqp->sqp/dot_general | solution.py:105
  141.9 0.0 copy-done
  141.9 0.0 copy-done.1
  141.9 0.0 copy-done.2
  142.0 54.1 %subtract_reduce_fusion = (f32[16,1024]{0,1:T(8,128)S(1)}, f32[16,1024]{0,1:T(8,128)S(1)}) fusion(f32[128]{0:T(128)S(1)} %convert_element_type.122, f32[1024,128]{1,0:T(8,128)S(1)} %copy-done.2, f32[16,128]{1,0:T(8,128)S(1)} %get-tuple-element.16, f32[128]{0:T(128)S(1)} %get-tuple-element.21, f32[128]{0:T(128)S(1)} %get-tuple-element.22, ...), kind=kOutput, calls=%fused_computation.1 | convolution fusion | flops 450858496 | bytes 35350020 | tf_op jit(solution)/shard_map/rs,rqp->sqp/dot_general | solution.py:106
  196.1 0.2 copy.46
  196.3 0.2 copy.45
  196.5 1.3 pad_maximum_fusion
  197.8 0.0 all-reduce.2.cloned.1.call-update
  197.8 140.7 %all-reduce.2.cloned.1.call-done = f32[32769]{0:T(1024)} async-done(((f32[32769]{0:T(1024)}), f32[32769]{0:T(1024)}) %all-reduce.2.cloned.1.call-update) | async-done | bytes 131092 | tf_op jit(solution)/shard_map/psum | solution.py:119
  338.5 0.9 fusion.125
  339.4 4.3 %fusion.31 = f32[16,160]{1,0:T(8,128)S(1)} fusion(f32[16,1024]{1,0:T(8,128)S(1)} %reshape.408, s32[160]{0:T(256)S(1)} %and_select_fusion), kind=kOutput, calls=%fused_computation.49 | convolution fusion | flops 33751040 | bytes 76416 | tf_op jit(solution)/shard_map/dot_general | solution.py:65
  343.8 4.4 %fusion.33 = f32[16,160]{1,0:T(8,128)S(1)} fusion(f32[16,1024]{1,0:T(8,128)S(1)} %reshape.408, s32[160]{0:T(256)S(1)} %and_select_fusion), kind=kOutput, calls=%fused_computation.50 | convolution fusion | flops 33751040 | bytes 76416 | tf_op jit(solution)/shard_map/dot_general | solution.py:68
  348.2 4.6 %convolution_subtract_fusion = f32[16,160]{1,0:T(8,128)S(1)} fusion(f32[16,160]{1,0:T(8,128)S(1)} %fusion.31, f32[16,1024]{1,0:T(8,128)S(1)} %reshape.409, s32[160]{0:T(256)S(1)} %and_select_fusion), kind=kOutput, calls=%fused_computation.34 | convolution fusion | flops 33753600 | bytes 86656 | tf_op jit(solution)/shard_map/dot_general | solution.py:65
  352.8 0.2 fusion.75
  353.0 4.4 %convolution_add_fusion = f32[16,160]{1,0:T(8,128)S(1)} fusion(f32[16,160]{1,0:T(8,128)S(1)} %fusion.33, f32[16,1024]{1,0:T(8,128)S(1)} %reshape.409, s32[160]{0:T(256)S(1)} %and_select_fusion), kind=kOutput, calls=%fused_computation.33 | convolution fusion | flops 33753600 | bytes 86656 | tf_op jit(solution)/shard_map/dot_general | solution.py:68
  357.3 0.2 fusion.73
  357.5 1.2 slice.40
  359.4 0.6 divide_multiply_fusion
  (15 shorter events, 0.2 us)
Async XLA Ops:
  6.5 18.4 %copy-start.5 = (s32[128]{0:T(128)S(1)}, s32[128]{0:T(128)}, u32[]{:S(2)}) copy-start(s32[128]{0:T(128)} %param.6) | copy-start | bytes 1540
  6.5 18.5 %copy-start.3 = (f32[2]{0:T(128)S(1)}, f32[2]{0:T(128)}, u32[]{:S(2)}) copy-start(f32[2]{0:T(128)} %param.7) | copy-start | bytes 28
  6.5 20.7 %copy-start.4 = (s32[128,2]{0,1:T(2,128)S(1)}, s32[128,2]{0,1:T(2,128)}, u32[]{:S(2)}) copy-start(s32[128,2]{0,1:T(2,128)} %param.5) | copy-start | bytes 3076
  12.9 63.8 %all-to-all-start = ((bf16[128,128,128]{1,2,0:T(8,128)(2,1)}), bf16[128,128,128]{1,2,0:T(8,128)(2,1)}, u32[]{:S(2)}, u32[]{:S(2)}) async-start(bf16[128,128,128]{1,2,0:T(8,128)(2,1)} %bitcast.61), calls=%async_computation | async-start | bytes 8388608 | tf_op jit(solution)/shard_map/all_to_all | solution.py:87
  24.9 313.6 %all-reduce.2.cloned.1.call-start = ((), (), s32[]{:S(2)}) async-start(), calls=%async_computation.1 | async-start | bytes 270336 | tf_op jit(solution)/shard_map/psum | solution.py:119
  125.3 16.7 %copy-start = (f32[16,1024,128]{2,0,1:T(8,128)S(1)}, f32[16,1024,128]{2,0,1:T(8,128)}, u32[]{:S(2)}) copy-start(f32[16,1024,128]{2,0,1:T(8,128)} %fusion.6) | copy-start | bytes 25165828
  125.3 16.7 %copy-start.1 = (f32[1024,128]{1,0:T(8,128)S(1)}, f32[1024,128]{1,0:T(8,128)}, u32[]{:S(2)}) copy-start(f32[1024,128]{1,0:T(8,128)} %get-tuple-element.11) | copy-start | bytes 1572868
  125.3 16.7 %copy-start.2 = (f32[1024,128]{1,0:T(8,128)S(1)}, f32[1024,128]{1,0:T(8,128)}, u32[]{:S(2)}) copy-start(f32[1024,128]{1,0:T(8,128)} %get-tuple-element.12) | copy-start | bytes 1572868
Sparse Core Ops, SparseCore 0:
  197.9 140.5 all-reduce.1
where the time goes:
time: 373 us; the launch traced here: 367 us
  waiting for transfers between devices  156 us (42%)
  matrix products  130 us (35%)
  other arithmetic  37.3 us (10%)
  local copies, waits for them, and re-layouts  16.7 us (4%)
  between operations  14.5 us (4%)
  starting transfers between devices  12 us (3%)
    psum x1, waiting for transfers between devices, local(): total = lax.psum(packed, ('scan', 'det'))  141 us
    dot_general x1, matrix products, local(): jnp.einsum('rs,rqp->sqp', row_cos, imag_col, precision=EXACT_PRECISION)  54.1 us
    neg x1, other arithmetic, local(): -col_sin  16.9 us
    dot_general x1, matrix products, local(): jnp.einsum('rs,rqp->sqp', row_sin, imag_col, precision=EXACT_PRECISION)  16.6 us
    dot_general x1, matrix products, local(): jnp.einsum('rs,rqp->sqp', row_cos, real_col, precision=EXACT_PRECISION)  16.6 us
    all_to_all x1, waiting for transfers between devices, local(): lax.all_to_all(blocks, ('scan', 'det'), split_axis=0, concat_axis=0, tile...  15.5 us
    convert_element_type x1, other arithmetic, local(): col_cos = jnp.cos(col_angles).astype(jnp.bfloat16)  15.5 us
    dot_general x1, matrix products, local(): jnp.einsum('abrcp,acq->brqp', images, table, preferred_element_type=jnp.f...  13.4 us
  transfers between devices with their start and end apart: 2, of which 2 were waited for; matrix products, arithmetic and copies ran while one was open for 10% of the time, Pallas kernels for 0%

commit v1 on v0

--- a/solution.py
+++ b/solution.py
@@ -11,6 +11,7 @@
 HALO = 16
 TWO_PI = 2.0 * math.pi
 EXACT_PRECISION = lax.Precision.HIGHEST
+_order_ranges = lambda field: lax.all_gather(field, ("scan", "det")).sum(axis=0)
 
 
 def phase_angles(first, second_operand, modulus):
@@ -116,7 +117,7 @@
     packed = jnp.concatenate(
         [spec_real.reshape(-1), spec_imag.reshape(-1), jnp.sum(weights).reshape(1)]
     )
-    total = lax.psum(packed, ("scan", "det"))
+    total = _order_ranges(packed)
     spec_real = total[: SR * SC].reshape(SR, SC)
     spec_imag = total[SR * SC : 2 * SR * SC].reshape(SR, SC)
     bright_sum = total[2 * SR * SC]

time: 373 us -> 483 us (1.29)
  waiting for transfers between devices: 156 us -> 230 us
  local copies, waits for them, and re-layouts: 16.7 us -> 44.5 us
  other arithmetic: 37.3 us -> 45.2 us
    unnamed x1 -> x2, waiting for transfers between devices: 0.02 us -> 215 us
    psum x1 -> x0, waiting for transfers between devices: 141 us -> none  [local(): total = lax.psum(packed, ('scan', 'det'))]
    all_gather x0 -> x1, local copies, waits for them, and re-layouts: none -> 23 us  [lax.all_gather(field, ('scan', 'det')).sum(axis=0)]
    reduce_sum x0 -> x1, other arithmetic: none -> 6.91 us  [lax.all_gather(field, ('scan', 'det')).sum(axis=0)]
    unnamed x15 -> x16, local copies, waits for them, and re-layouts: 6.47 us -> 12.8 us
  transfers between devices with their start and end apart: 2 -> 2, of which waited for: 2 -> 2; matrix products, arithmetic and copies ran while one was open for 10% -> 8% of each run, Pallas kernels for 0% -> 0%
where the time goes in v1:
time: 483 us; the launch traced here: 477 us
  waiting for transfers between devices  230 us (48%)
  matrix products  130 us (27%)
  other arithmetic  45.2 us (9%)
  local copies, waits for them, and re-layouts  44.5 us (9%)
  between operations  14.5 us (3%)
  starting transfers between devices  12 us (2%)
    unnamed x2, waiting for transfers between devices  215 us
    dot_general x1, matrix products, local(): jnp.einsum('rs,rqp->sqp', row_cos, imag_col, precision=EXACT_PRECISION)  53.6 us
    all_gather x1, local copies, waits for them, and re-layouts, lax.all_gather(field, ('scan', 'det')).sum(axis=0)  23 us
    neg x1, other arithmetic, local(): -col_sin  16.9 us
    dot_general x1, matrix products, local(): jnp.einsum('rs,rqp->sqp', row_cos, real_col, precision=EXACT_PRECISION)  16.9 us
    dot_general x1, matrix products, local(): jnp.einsum('rs,rqp->sqp', row_sin, imag_col, precision=EXACT_PRECISION)  16.6 us
    all_to_all x1, waiting for transfers between devices, local(): lax.all_to_all(blocks, ('scan', 'det'), split_axis=0, concat_axis=0, tile...  15.6 us
    convert_element_type x1, other arithmetic, local(): col_cos = jnp.cos(col_angles).astype(jnp.bfloat16)  15.5 us
  transfers between devices with their start and end apart: 2, of which 2 were waited for; matrix products, arithmetic and copies ran while one was open for 8% of the time, Pallas kernels for 0%

profile of v1, /device:TPU:1, one launch (start us, length us, event | category | flops | bytes accessed | tf_op | source)
XLA Modules:
  0.0 476.6 jit_solution(13541907222228300658)
XLA Ops:
  6.5 0.0 copy-start.5
  6.5 0.0 copy-start.3
  6.5 0.0 copy-start.4
  6.5 6.4 %copy.37 = bf16[1,128,16384]{1,2,0:T(8,128)(2,1)} copy(bf16[1,128,16384]{2,1,0:T(8,128)(2,1)} %param.4) | data formatting | bytes 8388608 | tf_op args[0]
  12.9 11.9 %all-to-all-start = ((bf16[128,128,128]{1,2,0:T(8,128)(2,1)}), bf16[128,128,128]{1,2,0:T(8,128)(2,1)}, u32[]{:S(2)}, u32[]{:S(2)}) async-start(bf16[128,128,128]{1,2,0:T(8,128)(2,1)} %bitcast.61), calls=%async_computation | async-start | bytes 8388608 | tf_op jit(solution)/shard_map/all_to_all | solution.py:88
  24.9 0.0 all-reduce.3.cloned.1.call-start
  24.9 0.0 copy-done.5
  25.0 0.0 copy-done.3
  25.0 0.6 fusion.126
  25.6 0.7 add_multiply_fusion.1
  26.3 0.2 copy.42
  26.6 0.6 convert_reduce_fusion
  27.2 0.0 copy-done.4
  27.2 0.1 add_multiply_fusion.2
  27.3 0.3 fusion.27
  27.6 1.2 add_multiply_fusion
  28.8 15.5 %cosine_convert_fusion = bf16[8,128,1024]{1,2,0:T(8,128)(2,1)S(1)} fusion(s32[8,128]{1,0:T(8,128)S(1)} %multiply_add_fusion), kind=kLoop, calls=%fused_computation.25 | loop fusion | flops 15728640 | bytes 2101248 | tf_op jit(solution)/shard_map/convert_element_type | solution.py:92
  44.3 16.9 %fusion.18 = bf16[8,128,1024]{1,2,0:T(8,128)(2,1)} fusion(s32[8,128]{1,0:T(8,128)S(1)} %multiply_add_fusion), kind=kLoop, calls=%fused_computation.29 | loop fusion | flops 18874368 | bytes 2101248 | tf_op jit(solution)/shard_map/neg | solution.py:94
  61.2 15.6 %all-to-all-done = bf16[128,128,128]{1,2,0:T(8,128)(2,1)} async-done(((bf16[128,128,128]{1,2,0:T(8,128)(2,1)}), bf16[128,128,128]{1,2,0:T(8,128)(2,1)}, u32[]{:S(2)}, u32[]{:S(2)}) %all-to-all-start) | async-done | bytes 4194336 | tf_op jit(solution)/shard_map/all_to_all | solution.py:88
  76.8 13.5 %convolution_bitcast_fusion = f32[16,2048,128]{2,1,0:T(8,128)} fusion(bf16[8,16,128,128]{2,3,1,0:T(8,128)(2,1)} %bitcast.5, bf16[8,128,1024]{1,2,0:T(8,128)(2,1)} %fusion.18, bf16[8,128,1024]{1,2,0:T(8,128)(2,1)S(1)} %cosine_convert_fusion), kind=kOutput, calls=%fused_computation.13 | convolution fusion | flops 8598323200 | bytes 25165824 | tf_op jit(solution)/shard_map/abrcp,acq->brqp/dot_general | solution.py:95
  90.2 7.0 %fusion.124 = (f32[16,1024,128]{2,1,0:T(8,128)S(1)}, f32[16,1024,128]{2,1,0:T(8,128)S(1)}) fusion(f32[16,2048,128]{2,1,0:T(8,128)} %convolution_bitcast_fusion), kind=kLoop, calls=%fused_computation.169 | loop fusion | bytes 33554432 | tf_op jit(solution)/shard_map/slice | solution.py:98
  97.3 11.6 %fusion.4 = f32[16,1024,128]{2,0,1:T(8,128)S(1)} fusion(f32[16,1024,128]{2,1,0:T(8,128)S(1)} %get-tuple-element.7), kind=kOutput, calls=%fused_computation.9 | convolution fusion | flops 402656768 | bytes 16777216 | tf_op jit(solution)/shard_map/rs,rqp->sqp/dot_general | solution.py:109
  108.9 16.9 %fusion.6 = f32[16,1024,128]{2,0,1:T(8,128)} fusion(f32[16,1024,128]{2,1,0:T(8,128)S(1)} %get-tuple-element.7), kind=kOutput, calls=%fused_computation.11 | convolution fusion | flops 402656768 | bytes 16777216 | tf_op jit(solution)/shard_map/rs,rqp->sqp/dot_general | solution.py:104
  125.8 0.0 copy-start
  125.8 0.0 copy-start.1
  125.8 0.0 copy-start.2
  125.8 16.6 %fusion.2 = f32[16,1024,128]{2,0,1:T(8,128)} fusion(f32[16,1024,128]{2,1,0:T(8,128)S(1)} %get-tuple-element.8), kind=kOutput, calls=%fused_computation.7 | convolution fusion | flops 402656768 | bytes 16777216 | tf_op jit(solution)/shard_map/rs,rqp->sqp/dot_general | solution.py:106
  142.3 0.0 copy-done
  142.3 0.0 copy-done.1
  142.3 0.0 copy-done.2
  142.3 53.6 %subtract_reduce_fusion = (f32[16,1024]{0,1:T(8,128)S(1)}, f32[16,1024]{0,1:T(8,128)S(1)}) fusion(f32[128]{0:T(128)S(1)} %convert_element_type.122, f32[1024,128]{1,0:T(8,128)S(1)} %copy-done.2, f32[16,128]{1,0:T(8,128)S(1)} %get-tuple-element.16, f32[128]{0:T(128)S(1)} %get-tuple-element.21, f32[128]{0:T(128)S(1)} %get-tuple-element.22, ...), kind=kOutput, calls=%fused_computation.1 | convolution fusion | flops 450858496 | bytes 35350020 | tf_op jit(solution)/shard_map/rs,rqp->sqp/dot_general | solution.py:107
  196.0 0.2 copy.45
  196.2 0.2 copy.46
  196.4 6.3 %broadcast.581 = f32[4194432]{0:T(1024)} broadcast(f32[]{:T(128)} %constant.163.clone.1), dimensions={} | broadcast | bytes 16777732
  202.7 2.3 maximum_dynamic-update-slice_fusion
  205.0 0.0 all-reduce.3.cloned.1.call-update
  205.1 214.6 %all-reduce.3.cloned.1.call-done = f32[4194432]{0:T(1024)} async-done(((f32[4194432]{0:T(1024)}), f32[4194432]{0:T(1024)}) %all-reduce.3.cloned.1.call-update) | async-done | bytes 16777744
  419.7 23.0 %reshape.411 = f32[128,32769]{1,0:T(8,128)} reshape(f32[4194432]{0:T(1024)} %all-reduce.3.cloned.1.call-done) | data formatting | bytes 33555456 | tf_op jit(solution)/shard_map/all_gather | solution.py:14
  442.7 6.9 %reduce_sum.39 = f32[32769]{0:T(1024)S(1)} reduce(f32[128,32769]{1,0:T(8,128)} %reshape.411, f32[]{:T(128)} %constant.163.clone.1), dimensions={0}, to_apply=%region_3.4 | reduce | flops 4161663 | bytes 16908808 | tf_op jit(solution)/shard_map/reduce_sum | solution.py:14
  449.6 0.5 slice.40
  450.2 4.4 fusion.33
  454.5 4.3 fusion.31
  459.6 4.6 convolution_subtract_fusion
  464.2 4.3 convolution_add_fusion
  468.5 0.2 fusion.73
  468.7 0.2 fusion.75
  468.9 0.6 divide_multiply_fusion
  (16 shorter events, 0.2 us)
Async XLA Ops:
  6.5 18.4 %copy-start.5 = (s32[128]{0:T(128)S(1)}, s32[128]{0:T(128)}, u32[]{:S(2)}) copy-start(s32[128]{0:T(128)} %param.6) | copy-start | bytes 1540
  6.5 18.5 %copy-start.3 = (f32[2]{0:T(128)S(1)}, f32[2]{0:T(128)}, u32[]{:S(2)}) copy-start(f32[2]{0:T(128)} %param.7) | copy-start | bytes 28
  6.5 20.7 %copy-start.4 = (s32[128,2]{0,1:T(2,128)S(1)}, s32[128,2]{0,1:T(2,128)}, u32[]{:S(2)}) copy-start(s32[128,2]{0,1:T(2,128)} %param.5) | copy-start | bytes 3076
  12.9 63.8 %all-to-all-start = ((bf16[128,128,128]{1,2,0:T(8,128)(2,1)}), bf16[128,128,128]{1,2,0:T(8,128)(2,1)}, u32[]{:S(2)}, u32[]{:S(2)}) async-start(bf16[128,128,128]{1,2,0:T(8,128)(2,1)} %bitcast.61), calls=%async_computation | async-start | bytes 8388608 | tf_op jit(solution)/shard_map/all_to_all | solution.py:88
  24.9 394.8 %all-reduce.3.cloned.1.call-start = ((), (), s32[]{:S(2)}) async-start(), calls=%async_computation.1 | async-start | bytes 33562624
  125.8 16.6 %copy-start = (f32[16,1024,128]{2,0,1:T(8,128)S(1)}, f32[16,1024,128]{2,0,1:T(8,128)}, u32[]{:S(2)}) copy-start(f32[16,1024,128]{2,0,1:T(8,128)} %fusion.6) | copy-start | bytes 25165828
  125.8 16.6 %copy-start.1 = (f32[1024,128]{1,0:T(8,128)S(1)}, f32[1024,128]{1,0:T(8,128)}, u32[]{:S(2)}) copy-start(f32[1024,128]{1,0:T(8,128)} %get-tuple-element.11) | copy-start | bytes 1572868
  125.8 16.6 %copy-start.2 = (f32[1024,128]{1,0:T(8,128)S(1)}, f32[1024,128]{1,0:T(8,128)}, u32[]{:S(2)}) copy-start(f32[1024,128]{1,0:T(8,128)} %get-tuple-element.12) | copy-start | bytes 1572868
Sparse Core Ops, SparseCore 0:
  205.2 214.4 all-reduce.2
